TPU v7x, 32 devices: a whole 2x2x4 slice. The times are simulated.
32 devices in a mesh: member: 2 (over x), row: 16 (over z, y, core).
Axes of the slice: x: 2, y: 2, z: 4, core: 2. Of those that a mesh axis runs over, the one named last changes fastest.
Arguments:
- coarse: bfloat16 [384, 128, 128], P('row', 'member'), parts along dimension 1, may hold values from -6 to 6
- skip_field: bfloat16 [192, 256, 256], P(None, ('member', 'row')), parts along dimension 1, may hold values from -6 to 6
- up_weight: bfloat16 [4, 4, 384, 192], replicated, may hold values from -0.15625 to 0.15625
- up_bias: float32 [192], replicated, may hold values from -3 to 3
- conv_weight: bfloat16 [3, 3, 384, 192], replicated, may hold values from -0.109375 to 0.109375
- conv_bias: float32 [192], replicated, may hold values from -3 to 3
Outputs:
- decoded: bfloat16 [192, 256, 256], P(None, ('member', 'row')), parts along dimension 1
There are 2 independent parts, one for each index of `member`. A program takes and returns all parts, laid end to end along the dimension named above; an argument that names none is the same for every part. Nothing has to cross between parts.
All inputs are finite; a program needn't handle non-finite values.
Results may differ from a plain program's by a relative error of at most 0.0055.
Values may be sent and summed in bfloat16 or wider, within the bound.
No kernel may reach another device: no remote copies, remote signals or barrier semaphores. Data moves between devices by JAX's collectives and lax.ppermute only.
A program may use at most 64 MiB of HBM per device.

v0:
```python
import jax
import jax.numpy as jnp
from jax import lax
from jax.sharding import PartitionSpec as P

TAP_TABLE = (((0, 3), (1, 1)), ((1, 2), (2, 0)))


def extended(x, sides, width):
    for axis, dim in sides:
        peers, length = (lax.axis_size(axis), x.shape[dim])
        up = [(i, (i + 1) % peers) for i in range(peers - 1)]
        down = [(j, i) for i, j in up]
        last = lax.slice_in_dim(x, length - width, length, axis=dim)
        initial = lax.slice_in_dim(x, 0, width, axis=dim)
        before = lax.ppermute(last, axis, up)
        after = lax.ppermute(initial, axis, down)
        x = jnp.concatenate([before, x, after], axis=dim)
    return x


def upsample(padded, weight):
    span_rows = padded.shape[1] - 2
    span_cols = padded.shape[2] - 2
    outputs = weight.shape[3]
    row_parts = []
    for row_par in range(2):
        col_parts = []
        for col_par in range(2):
            summed = jnp.zeros((outputs, span_rows, span_cols), jnp.float32)
            for row_off, row_tap in TAP_TABLE[row_par]:
                for col_off, col_tap in TAP_TABLE[col_par]:
                    window = padded[:, row_off : row_off + span_rows, col_off : col_off + span_cols]
                    summed = summed + jnp.einsum(
                        "chw,co->ohw",
                        window,
                        weight[row_tap, col_tap],
                        preferred_element_type=jnp.float32,
                    )
            col_parts.append(summed)
        row_parts.append(jnp.stack(col_parts, axis=-1))
    stacked = jnp.stack(row_parts, axis=2)
    return stacked.reshape(outputs, 2 * span_rows, 2 * span_cols)


def conv_taps(padded, weight):
    span_rows = padded.shape[1] - 2
    span_cols = padded.shape[2] - 2
    summed = jnp.zeros((weight.shape[3], span_rows, span_cols), jnp.float32)
    for row_tap in range(3):
        for col_tap in range(3):
            window = padded[:, row_tap : row_tap + span_rows, col_tap : col_tap + span_cols]
            summed = summed + jnp.einsum(
                "chw,co->ohw", window, weight[row_tap, col_tap], preferred_element_type=jnp.float32
            )
    return summed


def shards(coarse, skip_field, up_weight, up_bias, conv_weight, conv_bias):
    tiled_rows = lax.all_to_all(coarse, "row", split_axis=1, concat_axis=0, tiled=True)
    rimmed = extended(tiled_rows, (("row", 1),), 1)
    raised = upsample(jnp.pad(rimmed, ((0, 0), (0, 0), (1, 1))), up_weight)
    upsampled = (raised + up_bias[:, None, None]).astype(jnp.bfloat16)
    joined = jnp.concatenate([skip_field, upsampled], axis=0)
    rimmed_fine = extended(joined, (("row", 1),), 1)
    pre = conv_taps(jnp.pad(rimmed_fine, ((0, 0), (0, 0), (1, 1))), conv_weight)
    pre = pre + conv_bias[:, None, None]
    return jax.nn.silu(pre).astype(jnp.bfloat16)


def solution(mesh):
    in_specs = (P("row", "member", None), P(None, ("member", "row"), None), P(), P(), P(), P())
    out_specs = P(None, ("member", "row"), None)
    return jax.shard_map(shards, mesh=mesh, in_specs=in_specs, out_specs=out_specs, check_vma=False)
```

profile of v0, /device:TPU:5, one launch (start us, length us, event | category | flops | bytes accessed | tf_op | source)
XLA Modules:
  0.0 64.4 jit_solution(7071694644316420056)
XLA Ops:
  0.0 2.0 %copy.15 = bf16[24,64,128]{2,0,1:T(8,128)(2,1)} copy(bf16[24,64,128]{2,1,0:T(8,128)(2,1)} %param.6) | data formatting | bytes 786432 | tf_op args[0]
  2.0 6.7 %all-to-all-start = ((bf16[24,64,128]{2,0,1:T(8,128)(2,1)}), bf16[24,64,128]{2,0,1:T(8,128)(2,1)S(1)}, u32[]{:S(2)}, u32[]{:S(2)}) async-start(bf16[24,64,128]{2,0,1:T(8,128)(2,1)} %copy.15), calls=%async_computation | async-start | bytes 786432 | tf_op jit(solution)/shard_map/all_to_all | solution.py:60
  8.7 1.4 %copy.19 = bf16[192,8,256]{2,0,1:T(8,128)(2,1)S(1)} copy(bf16[192,8,256]{2,1,0:T(8,128)(2,1)} %param.7) | data formatting | bytes 1572864 | tf_op args[1]
  10.1 9.6 %all-to-all-done = bf16[24,64,128]{2,0,1:T(8,128)(2,1)S(1)} async-done(((bf16[24,64,128]{2,0,1:T(8,128)(2,1)}), bf16[24,64,128]{2,0,1:T(8,128)(2,1)S(1)}, u32[]{:S(2)}, u32[]{:S(2)}) %all-to-all-start) | async-done | bytes 393248 | tf_op jit(solution)/shard_map/all_to_all | solution.py:60
  19.8 0.3 fusion.75
  20.1 0.3 fusion.79
  20.4 0.3 fusion.83
  20.6 3.2 %collective-permute-start = (bf16[384,1,128]{2,0,1:T(8,128)(2,1)S(1)}, bf16[384,1,128]{2,0,1:T(8,128)(2,1)S(1)}, u32[]{:S(2)}, u32[]{:S(2)}) collective-permute-start(bf16[384,1,128]{2,0,1:T(8,128)(2,1)S(1)} %get-tuple-element.7), channel_id=1, source_target_pairs={{0,1},{1,2},{2,3},{3,4},{4,5},{5,6},{6,7},{7,8},{8,9},{9,10},{10,1... | collective-permute-start | bytes 294920 | tf_op jit(solution)/shard_map/ppermute | solution.py:16
  23.9 1.9 %collective-permute-start.1 = (bf16[384,1,128]{2,0,1:T(8,128)(2,1)S(1)}, bf16[384,1,128]{2,0,1:T(8,128)(2,1)S(1)}, u32[]{:S(2)}, u32[]{:S(2)}) collective-permute-start(bf16[384,1,128]{2,0,1:T(8,128)(2,1)S(1)} %get-tuple-element.8), channel_id=1, source_target_pairs={{1,0},{2,1},{3,2},{4,3},{5,4},{6,5},{7,6},{8,7},{9,8},{10,9},{11,1... | collective-permute-start | bytes 294920 | tf_op jit(solution)/shard_map/ppermute | solution.py:17
  25.8 0.3 fusion.87
  26.1 0.0 collective-permute-done
  26.1 4.6 %collective-permute-done.1 = bf16[384,1,128]{2,0,1:T(8,128)(2,1)S(1)} collective-permute-done((bf16[384,1,128]{2,0,1:T(8,128)(2,1)S(1)}, bf16[384,1,128]{2,0,1:T(8,128)(2,1)S(1)}, u32[]{:S(2)}, u32[]{:S(2)}) %collective-permute-start.1) | collective-permute-done | bytes 98336 | tf_op jit(solution)/shard_map/ppermute | solution.py:17
  30.7 0.6 fusion.48
  31.3 0.3 convolution_bitcast_fusion.4
  31.6 0.4 fusion.51
  32.0 0.3 convolution_bitcast_fusion.1
  32.2 0.4 fusion.45
  32.6 0.4 fusion.39
  33.0 0.3 fusion.58
  33.3 0.3 convolution_add_fusion.2
  33.6 0.3 fusion.44
  33.8 0.4 fusion.33
  34.2 0.3 fusion.43
  34.5 0.3 fusion.46
  34.8 0.3 fusion.36
  35.1 0.1 maximum_bitcast_fusion
  35.2 1.3 %pad_maximum_fusion.8 = f32[192,4,2,128,2]{3,0,1,4,2:T(8,128)} fusion(f32[192,4,1,128,2]{3,0,1,4,2:T(8,128)S(1)} %get-tuple-element.10, f32[192,4,1,128,2]{3,0,1,4,2:T(8,128)S(1)} %get-tuple-element.9), kind=kLoop, calls=%fused_computation.31 | loop fusion | flops 393216 | bytes 3145728 | tf_op jit(solution)/shard_map/stack | solution.py:42
  36.5 2.8 %copy.17 = f32[192,4,2,128,2]{0,4,3,2,1:T(2,128)S(1)} copy(f32[192,4,2,128,2]{3,0,1,4,2:T(8,128)} %pad_maximum_fusion.8) | data formatting | bytes 3145728 | tf_op jit(solution)/shard_map/stack | solution.py:42
  39.3 2.5 %reshape.5 = f32[192,8,256]{0,2,1:T(8,128)} reshape(f32[192,4,2,128,2]{0,4,3,2,1:T(2,128)S(1)} %copy.17) | data formatting | bytes 3145728 | tf_op jit(solution)/shard_map/reshape | solution.py:43
  41.7 1.9 %copy.18 = f32[192,8,256]{2,0,1:T(8,128)S(1)} copy(f32[192,8,256]{0,2,1:T(8,128)} %reshape.5) | data formatting | bytes 3145728 | tf_op jit(solution)/shard_map/reshape | solution.py:43
  43.7 0.2 add_convert_fusion
  43.8 0.0 copy-start.1
  43.9 2.1 %collective-permute-start.2 = (bf16[384,1,256]{2,0,1:T(8,128)(2,1)S(1)}, bf16[384,1,256]{2,0,1:T(8,128)(2,1)S(1)}, u32[]{:S(2)}, u32[]{:S(2)}) collective-permute-start(bf16[384,1,256]{2,0,1:T(8,128)(2,1)S(1)} %get-tuple-element.5), channel_id=1, source_target_pairs={{0,1},{1,2},{2,3},{3,4},{4,5},{5,6},{6,7},{7,8},{8,9},{9,10},{10,1... | collective-permute-start | bytes 589832 | tf_op jit(solution)/shard_map/ppermute | solution.py:16
  45.9 2.6 %collective-permute-start.3 = (bf16[384,1,256]{2,0,1:T(8,128)(2,1)S(1)}, bf16[384,1,256]{2,0,1:T(8,128)(2,1)S(1)}, u32[]{:S(2)}, u32[]{:S(2)}) collective-permute-start(bf16[384,1,256]{2,0,1:T(8,128)(2,1)S(1)} %get-tuple-element.6), channel_id=1, source_target_pairs={{1,0},{2,1},{3,2},{4,3},{5,4},{6,5},{7,6},{8,7},{9,8},{10,9},{11,1... | collective-permute-start | bytes 589832 | tf_op jit(solution)/shard_map/ppermute | solution.py:17
  48.5 0.6 fusion.21
  49.1 4.7 %collective-permute-done.3 = bf16[384,1,256]{2,0,1:T(8,128)(2,1)S(1)} collective-permute-done((bf16[384,1,256]{2,0,1:T(8,128)(2,1)S(1)}, bf16[384,1,256]{2,0,1:T(8,128)(2,1)S(1)}, u32[]{:S(2)}, u32[]{:S(2)}) %collective-permute-start.3) | collective-permute-done | bytes 196640 | tf_op jit(solution)/shard_map/ppermute | solution.py:17
  53.8 3.5 %select_maximum_fusion = bf16[384,10,258]{2,0,1:T(8,128)(2,1)S(1)} fusion(bf16[384,1,256]{2,0,1:T(8,128)(2,1)S(1)} %collective-permute-done.3, bf16[384,1,256]{2,0,1:T(8,128)(2,1)S(1)} %collective-permute-done.2, bf16[192,8,256]{2,0,1:T(8,128)(2,1)S(1)} %add_convert_fusion, bf16[192,8,256]{2,0,1:T(8,128)(2,1)S(1)} %copy.19), kind=kLoop, calls=%fused_computation.5 | loop fusion | flops 14860800 | bytes 3947520 | tf_op jit(solution)/shard_map/concatenate | solution.py:18
  57.3 0.6 fusion.9
  57.9 0.7 %fusion.11 = f32[8,256,192]{1,2,0:T(8,128)S(1)} fusion(bf16[384,10,258]{2,0,1:T(8,128)(2,1)S(1)} %select_maximum_fusion, bf16[3,3,384,192]{2,3,1,0:T(8,128)(2,1)S(1)} %copy-done.1), kind=kOutput, calls=%fused_computation.19 | convolution fusion | flops 301989888 | bytes 3293184 | tf_op jit(solution)/shard_map/chw,co->ohw/dot_general | solution.py:53
  58.6 0.6 fusion.13
  59.2 0.7 %fusion.15 = f32[8,256,192]{1,2,0:T(8,128)S(1)} fusion(bf16[384,10,258]{2,0,1:T(8,128)(2,1)S(1)} %select_maximum_fusion, bf16[3,3,384,192]{2,3,1,0:T(8,128)(2,1)S(1)} %copy-done.1), kind=kOutput, calls=%fused_computation.23 | convolution fusion | flops 301989888 | bytes 3293184 | tf_op jit(solution)/shard_map/chw,co->ohw/dot_general | solution.py:53
  59.9 0.6 fusion.19
  60.5 0.6 fusion.7
  61.1 0.0 copy-start.3
  61.1 0.6 fusion.17
  61.7 0.1 copy-done.3
  61.7 1.4 %fusion.28 = bf16[192,8,256]{2,0,1:T(8,128)(2,1)S(1)} fusion(f32[8,256,192]{1,2,0:T(8,128)S(1)} %fusion.7, f32[8,256,192]{1,2,0:T(8,128)S(1)} %fusion.9, f32[8,256,192]{1,2,0:T(8,128)S(1)} %fusion.11, f32[8,256,192]{1,2,0:T(8,128)S(1)} %fusion.21, f32[8,256,192]{1,2,0:T(8,128)S(1)} %fusion.13, f32[8,256,192]{1,2,0:T(8,128)S(1)} %fusion.15, ...), kind=kOutput, calls=%fused_computation.42 | convolution fusion | flops 307494912 | bytes 15090688 | tf_op jit(solution)/shard_map/chw,co->ohw/dot_general | solution.py:53
  63.1 1.3 %copy.20 = bf16[192,8,256]{2,1,0:T(8,128)(2,1)} copy(bf16[192,8,256]{2,0,1:T(8,128)(2,1)S(1)} %fusion.28) | data formatting | bytes 1572864 | tf_op jit(solution)/shard_map/convert_element_type | solution.py:68
  (9 shorter events, 0.1 us)
Async XLA Ops:
  2.0 17.7 %all-to-all-start = ((bf16[24,64,128]{2,0,1:T(8,128)(2,1)}), bf16[24,64,128]{2,0,1:T(8,128)(2,1)S(1)}, u32[]{:S(2)}, u32[]{:S(2)}) async-start(bf16[24,64,128]{2,0,1:T(8,128)(2,1)} %copy.15), calls=%async_computation | async-start | bytes 786432 | tf_op jit(solution)/shard_map/all_to_all | solution.py:60
  8.7 11.2 %copy-start = (bf16[4,4,384,192]{2,3,1,0:T(8,128)(2,1)S(1)}, bf16[4,4,384,192]{2,3,1,0:T(8,128)(2,1)}, u32[]{:S(2)}) copy-start(bf16[4,4,384,192]{2,3,1,0:T(8,128)(2,1)} %param.8) | copy-start | bytes 7077892
  20.6 5.5 %collective-permute-start = (bf16[384,1,128]{2,0,1:T(8,128)(2,1)S(1)}, bf16[384,1,128]{2,0,1:T(8,128)(2,1)S(1)}, u32[]{:S(2)}, u32[]{:S(2)}) collective-permute-start(bf16[384,1,128]{2,0,1:T(8,128)(2,1)S(1)} %get-tuple-element.7), channel_id=1, source_target_pairs={{0,1},{1,2},{2,3},{3,4},{4,5},{5,6},{6,7},{7,8},{8,9},{9,10},{10,1... | collective-permute-start | bytes 294920 | tf_op jit(solution)/shard_map/ppermute | solution.py:16
  23.9 6.8 %collective-permute-start.1 = (bf16[384,1,128]{2,0,1:T(8,128)(2,1)S(1)}, bf16[384,1,128]{2,0,1:T(8,128)(2,1)S(1)}, u32[]{:S(2)}, u32[]{:S(2)}) collective-permute-start(bf16[384,1,128]{2,0,1:T(8,128)(2,1)S(1)} %get-tuple-element.8), channel_id=1, source_target_pairs={{1,0},{2,1},{3,2},{4,3},{5,4},{6,5},{7,6},{8,7},{9,8},{10,9},{11,1... | collective-permute-start | bytes 294920 | tf_op jit(solution)/shard_map/ppermute | solution.py:17
  41.7 1.9 %copy-start.2 = (f32[192]{0:T(256)S(1)}, f32[192]{0:T(256)}, u32[]{:S(2)}) copy-start(f32[192]{0:T(256)} %param.9) | copy-start | bytes 2308
  43.8 4.7 %copy-start.1 = (bf16[3,3,384,192]{2,3,1,0:T(8,128)(2,1)S(1)}, bf16[3,3,384,192]{2,3,1,0:T(8,128)(2,1)}, u32[]{:S(2)}) copy-start(bf16[3,3,384,192]{2,3,1,0:T(8,128)(2,1)} %param.10) | copy-start | bytes 3981316
  43.9 5.2 %collective-permute-start.2 = (bf16[384,1,256]{2,0,1:T(8,128)(2,1)S(1)}, bf16[384,1,256]{2,0,1:T(8,128)(2,1)S(1)}, u32[]{:S(2)}, u32[]{:S(2)}) collective-permute-start(bf16[384,1,256]{2,0,1:T(8,128)(2,1)S(1)} %get-tuple-element.5), channel_id=1, source_target_pairs={{0,1},{1,2},{2,3},{3,4},{4,5},{5,6},{6,7},{7,8},{8,9},{9,10},{10,1... | collective-permute-start | bytes 589832 | tf_op jit(solution)/shard_map/ppermute | solution.py:16
  45.9 7.9 %collective-permute-start.3 = (bf16[384,1,256]{2,0,1:T(8,128)(2,1)S(1)}, bf16[384,1,256]{2,0,1:T(8,128)(2,1)S(1)}, u32[]{:S(2)}, u32[]{:S(2)}) collective-permute-start(bf16[384,1,256]{2,0,1:T(8,128)(2,1)S(1)} %get-tuple-element.6), channel_id=1, source_target_pairs={{1,0},{2,1},{3,2},{4,3},{5,4},{6,5},{7,6},{8,7},{9,8},{10,9},{11,1... | collective-permute-start | bytes 589832 | tf_op jit(solution)/shard_map/ppermute | solution.py:17
  61.1 0.7 %copy-start.3 = (f32[192]{0:T(256)S(1)}, f32[192]{0:T(256)}, u32[]{:S(2)}) copy-start(f32[192]{0:T(256)} %param.11) | copy-start | bytes 2308
where the time goes:
time: 64.9 us; the launch traced here: 64.4 us
  waiting for transfers between devices  19 us (29%)
  starting transfers between devices  16.5 us (25%)
  local copies, waits for them, and re-layouts  12 us (18%)
  matrix products  10.9 us (17%)
  other arithmetic  5.71 us (9%)
    all_to_all x1, waiting for transfers between devices, shards(): lax.all_to_all(coarse, 'row', split_axis=1, concat_axis=0, tiled=True)  9.63 us
    ppermute x2, waiting for transfers between devices, extended(): after = lax.ppermute(initial, axis, down)  9.32 us
    all_to_all x1, starting transfers between devices, shards(): lax.all_to_all(coarse, 'row', split_axis=1, concat_axis=0, tiled=True)  6.67 us
    dot_general x9, matrix products, conv_taps(): jnp.einsum('chw,co->ohw', window, weight[row_tap, col_tap], preferred_ele...  6.21 us
    ppermute x2, starting transfers between devices, extended(): before = lax.ppermute(last, axis, up)  5.3 us
    dot_general x16, matrix products, upsample(): jnp.einsum('chw,co->ohw', window, weight[row_tap, col_tap], preferred_ele...  4.71 us
    ppermute x2, starting transfers between devices, extended(): after = lax.ppermute(initial, axis, down)  4.51 us
    reshape x2, local copies, waits for them, and re-layouts, upsample(): return stacked.reshape(outputs, 2 * span_rows, 2 * span_cols)  4.37 us
  transfers between devices with their start and end apart: 5, of which 3 were waited for; matrix products, arithmetic and copies ran while one was open for 4% of the time, Pallas kernels for 0%

commit v1 on v0

--- a/solution.py
+++ b/solution.py
@@ -57,7 +57,10 @@
 
 
 def shards(coarse, skip_field, up_weight, up_bias, conv_weight, conv_bias):
-    tiled_rows = lax.all_to_all(coarse, "row", split_axis=1, concat_axis=0, tiled=True)
+    tiled_rows = jnp.concatenate(
+        lax.all_to_all(jnp.stack(jnp.split(coarse, lax.axis_size("row"), axis=1)), "row", 0, 0),
+        axis=0,
+    )
     rimmed = extended(tiled_rows, (("row", 1),), 1)
     raised = upsample(jnp.pad(rimmed, ((0, 0), (0, 0), (1, 1))), up_weight)
     upsampled = (raised + up_bias[:, None, None]).astype(jnp.bfloat16)

time: 64.9 us -> 86.4 us (1.33)
  local copies, waits for them, and re-layouts: 12 us -> 32.7 us
    unnamed x10 -> x24, local copies, waits for them, and re-layouts: 3.54 us -> 22.8 us
    another operation x0 -> x1, local copies, waits for them, and re-layouts: none -> 1.42 us  [shards(): jnp.stack(jnp.split(coarse, lax.axis_size('row'), axis=1))]
  transfers between devices with their start and end apart: 5 -> 5, of which waited for: 3 -> 3; matrix products, arithmetic and copies ran while one was open for 4% -> 3% of each run, Pallas kernels for 0% -> 0%
where the time goes in v1:
time: 86.4 us; the launch traced here: 85.1 us
  local copies, waits for them, and re-layouts  32.7 us (38%)
  waiting for transfers between devices  19 us (22%)
  starting transfers between devices  16.5 us (19%)
  matrix products  10.9 us (13%)
  other arithmetic  5.71 us (7%)
    unnamed x24, local copies, waits for them, and re-layouts  22.8 us
    all_to_all x1, waiting for transfers between devices, shards(): lax.all_to_all(jnp.stack(jnp.split(coarse, lax.axis_size('row'), axis=1))...  9.63 us
    ppermute x2, waiting for transfers between devices, extended(): after = lax.ppermute(initial, axis, down)  9.32 us
    all_to_all x1, starting transfers between devices, shards(): lax.all_to_all(jnp.stack(jnp.split(coarse, lax.axis_size('row'), axis=1))...  6.67 us
    dot_general x9, matrix products, conv_taps(): jnp.einsum('chw,co->ohw', window, weight[row_tap, col_tap], preferred_ele...  6.22 us
    ppermute x2, starting transfers between devices, extended(): before = lax.ppermute(last, axis, up)  5.29 us
    dot_general x16, matrix products, upsample(): jnp.einsum('chw,co->ohw', window, weight[row_tap, col_tap], preferred_ele...  4.66 us
    ppermute x2, starting transfers between devices, extended(): after = lax.ppermute(initial, axis, down)  4.51 us
  transfers between devices with their start and end apart: 5, of which 3 were waited for; matrix products, arithmetic and copies ran while one was open for 3% of the time, Pallas kernels for 0%

profile of v1, /device:TPU:5, one launch (start us, length us, event | category | flops | bytes accessed | tf_op | source)
XLA Modules:
  0.0 85.1 jit_solution(8967099502651148419)
XLA Ops:
  0.0 1.4 %constant_dynamic-update-slice_fusion.15 = bf16[16,24,4,128]{3,2,1,0:T(4,128)(2,1)} fusion(bf16[24,64,128]{2,1,0:T(8,128)(2,1)} %param.6), kind=kLoop, calls=%fused_computation.149 | loop fusion | bytes 49152
  1.4 1.4 %constant_dynamic-update-slice_fusion.14 = bf16[16,24,4,128]{3,2,1,0:T(4,128)(2,1)} fusion(bf16[16,24,4,128]{3,2,1,0:T(4,128)(2,1)} %constant_dynamic-update-slice_fusion.15, bf16[24,64,128]{2,1,0:T(8,128)(2,1)} %param.6), kind=kLoop, calls=%fused_computation.148 | loop fusion | bytes 49152
  2.8 1.4 %constant_dynamic-update-slice_fusion.13 = bf16[16,24,4,128]{3,2,1,0:T(4,128)(2,1)} fusion(bf16[16,24,4,128]{3,2,1,0:T(4,128)(2,1)} %constant_dynamic-update-slice_fusion.14, bf16[24,64,128]{2,1,0:T(8,128)(2,1)} %param.6), kind=kLoop, calls=%fused_computation.147 | loop fusion | bytes 49152
  4.2 1.4 %constant_dynamic-update-slice_fusion.12 = bf16[16,24,4,128]{3,2,1,0:T(4,128)(2,1)} fusion(bf16[16,24,4,128]{3,2,1,0:T(4,128)(2,1)} %constant_dynamic-update-slice_fusion.13, bf16[24,64,128]{2,1,0:T(8,128)(2,1)} %param.6), kind=kLoop, calls=%fused_computation.146 | loop fusion | bytes 49152
  5.7 1.4 %constant_dynamic-update-slice_fusion.11 = bf16[16,24,4,128]{3,2,1,0:T(4,128)(2,1)} fusion(bf16[16,24,4,128]{3,2,1,0:T(4,128)(2,1)} %constant_dynamic-update-slice_fusion.12, bf16[24,64,128]{2,1,0:T(8,128)(2,1)} %param.6), kind=kLoop, calls=%fused_computation.145 | loop fusion | bytes 49152
  7.1 1.4 %constant_dynamic-update-slice_fusion.10 = bf16[16,24,4,128]{3,2,1,0:T(4,128)(2,1)} fusion(bf16[16,24,4,128]{3,2,1,0:T(4,128)(2,1)} %constant_dynamic-update-slice_fusion.11, bf16[24,64,128]{2,1,0:T(8,128)(2,1)} %param.6), kind=kLoop, calls=%fused_computation.144 | loop fusion | bytes 49152
  8.5 1.4 %constant_dynamic-update-slice_fusion.9 = bf16[16,24,4,128]{3,2,1,0:T(4,128)(2,1)} fusion(bf16[16,24,4,128]{3,2,1,0:T(4,128)(2,1)} %constant_dynamic-update-slice_fusion.10, bf16[24,64,128]{2,1,0:T(8,128)(2,1)} %param.6), kind=kLoop, calls=%fused_computation.143 | loop fusion | bytes 49152
  9.9 1.4 %constant_dynamic-update-slice_fusion.8 = bf16[16,24,4,128]{3,2,1,0:T(4,128)(2,1)} fusion(bf16[16,24,4,128]{3,2,1,0:T(4,128)(2,1)} %constant_dynamic-update-slice_fusion.9, bf16[24,64,128]{2,1,0:T(8,128)(2,1)} %param.6), kind=kLoop, calls=%fused_computation.142 | loop fusion | bytes 49152
  11.3 1.4 %constant_dynamic-update-slice_fusion.7 = bf16[16,24,4,128]{3,2,1,0:T(4,128)(2,1)} fusion(bf16[16,24,4,128]{3,2,1,0:T(4,128)(2,1)} %constant_dynamic-update-slice_fusion.8, bf16[24,64,128]{2,1,0:T(8,128)(2,1)} %param.6), kind=kLoop, calls=%fused_computation.141 | loop fusion | bytes 49152
  12.8 1.4 %constant_dynamic-update-slice_fusion.6 = bf16[16,24,4,128]{3,2,1,0:T(4,128)(2,1)} fusion(bf16[16,24,4,128]{3,2,1,0:T(4,128)(2,1)} %constant_dynamic-update-slice_fusion.7, bf16[24,64,128]{2,1,0:T(8,128)(2,1)} %param.6), kind=kLoop, calls=%fused_computation.140 | loop fusion | bytes 49152
  14.2 1.4 %constant_dynamic-update-slice_fusion.5 = bf16[16,24,4,128]{3,2,1,0:T(4,128)(2,1)} fusion(bf16[16,24,4,128]{3,2,1,0:T(4,128)(2,1)} %constant_dynamic-update-slice_fusion.6, bf16[24,64,128]{2,1,0:T(8,128)(2,1)} %param.6), kind=kLoop, calls=%fused_computation.139 | loop fusion | bytes 49152
  15.6 1.4 %constant_dynamic-update-slice_fusion.4 = bf16[16,24,4,128]{3,2,1,0:T(4,128)(2,1)} fusion(bf16[16,24,4,128]{3,2,1,0:T(4,128)(2,1)} %constant_dynamic-update-slice_fusion.5, bf16[24,64,128]{2,1,0:T(8,128)(2,1)} %param.6), kind=kLoop, calls=%fused_computation.138 | loop fusion | bytes 49152
  17.0 1.4 %constant_dynamic-update-slice_fusion.3 = bf16[16,24,4,128]{3,2,1,0:T(4,128)(2,1)} fusion(bf16[16,24,4,128]{3,2,1,0:T(4,128)(2,1)} %constant_dynamic-update-slice_fusion.4, bf16[24,64,128]{2,1,0:T(8,128)(2,1)} %param.6), kind=kLoop, calls=%fused_computation.137 | loop fusion | bytes 49152
  18.4 1.4 %constant_dynamic-update-slice_fusion.2 = bf16[16,24,4,128]{3,2,1,0:T(4,128)(2,1)} fusion(bf16[16,24,4,128]{3,2,1,0:T(4,128)(2,1)} %constant_dynamic-update-slice_fusion.3, bf16[24,64,128]{2,1,0:T(8,128)(2,1)} %param.6), kind=kLoop, calls=%fused_computation.136 | loop fusion | bytes 49152
  19.8 1.4 %constant_dynamic-update-slice_fusion.1 = bf16[16,24,4,128]{3,2,1,0:T(4,128)(2,1)} fusion(bf16[16,24,4,128]{3,2,1,0:T(4,128)(2,1)} %constant_dynamic-update-slice_fusion.2, bf16[24,64,128]{2,1,0:T(8,128)(2,1)} %param.6), kind=kLoop, calls=%fused_computation.135 | loop fusion | bytes 49152
  21.3 1.4 %constant_dynamic-update-slice_fusion = bf16[16,24,4,128]{3,2,1,0:T(4,128)(2,1)} fusion(bf16[16,24,4,128]{3,2,1,0:T(4,128)(2,1)} %constant_dynamic-update-slice_fusion.1, bf16[24,64,128]{2,1,0:T(8,128)(2,1)} %param.6), kind=kLoop, calls=%fused_computation.134 | loop fusion | bytes 49152 | tf_op jit(solution)/shard_map/stack | solution.py:61
  22.7 6.7 %all-to-all-start = ((bf16[16,24,4,128]{3,2,1,0:T(4,128)(2,1)}), bf16[16,24,4,128]{3,2,1,0:T(4,128)(2,1)S(1)}, u32[]{:S(2)}, u32[]{:S(2)}) async-start(bf16[16,24,4,128]{3,2,1,0:T(4,128)(2,1)} %constant_dynamic-update-slice_fusion), calls=%async_computation | async-start | bytes 786432 | tf_op jit(solution)/shard_map/all_to_all | solution.py:61
  29.4 1.4 %copy.13 = bf16[192,8,256]{2,0,1:T(8,128)(2,1)S(1)} copy(bf16[192,8,256]{2,1,0:T(8,128)(2,1)} %param.7) | data formatting | bytes 1572864 | tf_op args[1]
  30.8 9.6 %all-to-all-done = bf16[16,24,4,128]{3,2,1,0:T(4,128)(2,1)S(1)} async-done(((bf16[16,24,4,128]{3,2,1,0:T(4,128)(2,1)}), bf16[16,24,4,128]{3,2,1,0:T(4,128)(2,1)S(1)}, u32[]{:S(2)}, u32[]{:S(2)}) %all-to-all-start) | async-done | bytes 393248 | tf_op jit(solution)/shard_map/all_to_all | solution.py:61
  41.1 3.2 %collective-permute-start = (bf16[384,1,128]{2,0,1:T(8,128)(2,1)S(1)}, bf16[384,1,128]{2,0,1:T(8,128)(2,1)S(1)}, u32[]{:S(2)}, u32[]{:S(2)}) collective-permute-start(bf16[384,1,128]{2,0,1:T(8,128)(2,1)S(1)} %get-tuple-element.7), channel_id=1, source_target_pairs={{0,1},{1,2},{2,3},{3,4},{4,5},{5,6},{6,7},{7,8},{8,9},{9,10},{10,1... | collective-permute-start | bytes 294920 | tf_op jit(solution)/shard_map/ppermute | solution.py:16
  44.3 1.9 %collective-permute-start.1 = (bf16[384,1,128]{2,0,1:T(8,128)(2,1)S(1)}, bf16[384,1,128]{2,0,1:T(8,128)(2,1)S(1)}, u32[]{:S(2)}, u32[]{:S(2)}) collective-permute-start(bf16[384,1,128]{2,0,1:T(8,128)(2,1)S(1)} %get-tuple-element.8), channel_id=1, source_target_pairs={{1,0},{2,1},{3,2},{4,3},{5,4},{6,5},{7,6},{8,7},{9,8},{10,9},{11,1... | collective-permute-start | bytes 294920 | tf_op jit(solution)/shard_map/ppermute | solution.py:17
  46.5 4.6 %collective-permute-done.1 = bf16[384,1,128]{2,0,1:T(8,128)(2,1)S(1)} collective-permute-done((bf16[384,1,128]{2,0,1:T(8,128)(2,1)S(1)}, bf16[384,1,128]{2,0,1:T(8,128)(2,1)S(1)}, u32[]{:S(2)}, u32[]{:S(2)}) %collective-permute-start.1) | collective-permute-done | bytes 98336 | tf_op jit(solution)/shard_map/ppermute | solution.py:17
  51.1 0.6 fusion.39
  51.7 0.4 fusion.43
  52.1 0.4 fusion.40
  52.5 0.4 convolution_add_fusion.1
  54.2 0.3 fusion.34
  54.5 0.3 fusion.35
  54.8 0.4 fusion.33
  55.2 0.3 fusion.32
  55.9 1.3 %pad_maximum_fusion.8 = f32[192,4,2,128,2]{3,0,1,4,2:T(8,128)} fusion(f32[192,4,1,128,2]{3,0,1,4,2:T(8,128)S(1)} %get-tuple-element.10, f32[192,4,1,128,2]{3,0,1,4,2:T(8,128)S(1)} %get-tuple-element.9), kind=kLoop, calls=%fused_computation.31 | loop fusion | flops 393216 | bytes 3145728 | tf_op jit(solution)/shard_map/stack | solution.py:42
  57.1 2.8 %copy.11 = f32[192,4,2,128,2]{0,4,3,2,1:T(2,128)S(1)} copy(f32[192,4,2,128,2]{3,0,1,4,2:T(8,128)} %pad_maximum_fusion.8) | data formatting | bytes 3145728 | tf_op jit(solution)/shard_map/stack | solution.py:42
  59.9 2.5 %reshape.9 = f32[192,8,256]{0,2,1:T(8,128)} reshape(f32[192,4,2,128,2]{0,4,3,2,1:T(2,128)S(1)} %copy.11) | data formatting | bytes 3145728 | tf_op jit(solution)/shard_map/reshape | solution.py:43
  62.4 1.9 %copy.12 = f32[192,8,256]{2,0,1:T(8,128)S(1)} copy(f32[192,8,256]{0,2,1:T(8,128)} %reshape.9) | data formatting | bytes 3145728 | tf_op jit(solution)/shard_map/reshape | solution.py:43
  64.5 2.1 %collective-permute-start.2 = (bf16[384,1,256]{2,0,1:T(8,128)(2,1)S(1)}, bf16[384,1,256]{2,0,1:T(8,128)(2,1)S(1)}, u32[]{:S(2)}, u32[]{:S(2)}) collective-permute-start(bf16[384,1,256]{2,0,1:T(8,128)(2,1)S(1)} %get-tuple-element.5), channel_id=1, source_target_pairs={{0,1},{1,2},{2,3},{3,4},{4,5},{5,6},{6,7},{7,8},{8,9},{9,10},{10,1... | collective-permute-start | bytes 589832 | tf_op jit(solution)/shard_map/ppermute | solution.py:16
  66.6 2.6 %collective-permute-start.3 = (bf16[384,1,256]{2,0,1:T(8,128)(2,1)S(1)}, bf16[384,1,256]{2,0,1:T(8,128)(2,1)S(1)}, u32[]{:S(2)}, u32[]{:S(2)}) collective-permute-start(bf16[384,1,256]{2,0,1:T(8,128)(2,1)S(1)} %get-tuple-element.6), channel_id=1, source_target_pairs={{1,0},{2,1},{3,2},{4,3},{5,4},{6,5},{7,6},{8,7},{9,8},{10,9},{11,1... | collective-permute-start | bytes 589832 | tf_op jit(solution)/shard_map/ppermute | solution.py:17
  69.2 0.6 fusion.21
  69.8 4.7 %collective-permute-done.3 = bf16[384,1,256]{2,0,1:T(8,128)(2,1)S(1)} collective-permute-done((bf16[384,1,256]{2,0,1:T(8,128)(2,1)S(1)}, bf16[384,1,256]{2,0,1:T(8,128)(2,1)S(1)}, u32[]{:S(2)}, u32[]{:S(2)}) %collective-permute-start.3) | collective-permute-done | bytes 196640 | tf_op jit(solution)/shard_map/ppermute | solution.py:17
  74.5 3.5 %select_maximum_fusion = bf16[384,10,258]{2,0,1:T(8,128)(2,1)S(1)} fusion(bf16[384,1,256]{2,0,1:T(8,128)(2,1)S(1)} %collective-permute-done.3, bf16[384,1,256]{2,0,1:T(8,128)(2,1)S(1)} %collective-permute-done.2, bf16[192,8,256]{2,0,1:T(8,128)(2,1)S(1)} %add_convert_fusion, bf16[192,8,256]{2,0,1:T(8,128)(2,1)S(1)} %copy.13), kind=kLoop, calls=%fused_computation.5 | loop fusion | flops 14860800 | bytes 3947520 | tf_op jit(solution)/shard_map/concatenate | solution.py:18
  78.0 0.6 fusion.9
  78.6 0.7 fusion.11
  79.3 0.6 fusion.13
  79.8 0.7 fusion.15
  80.6 0.6 fusion.19
  81.1 0.6 fusion.7
  81.7 0.6 fusion.17
  82.4 1.4 %fusion.28 = bf16[192,8,256]{2,0,1:T(8,128)(2,1)S(1)} fusion(f32[8,256,192]{1,2,0:T(8,128)S(1)} %fusion.7, f32[8,256,192]{1,2,0:T(8,128)S(1)} %fusion.9, f32[8,256,192]{1,2,0:T(8,128)S(1)} %fusion.11, f32[8,256,192]{1,2,0:T(8,128)S(1)} %fusion.21, f32[8,256,192]{1,2,0:T(8,128)S(1)} %fusion.13, f32[8,256,192]{1,2,0:T(8,128)S(1)} %fusion.15, ...), kind=kOutput, calls=%fused_computation.42 | convolution fusion | flops 307494912 | bytes 15090688 | tf_op jit(solution)/shard_map/chw,co->ohw/dot_general | solution.py:53
  83.8 1.3 %copy.14 = bf16[192,8,256]{2,1,0:T(8,128)(2,1)} copy(bf16[192,8,256]{2,0,1:T(8,128)(2,1)S(1)} %fusion.28) | data formatting | bytes 1572864 | tf_op jit(solution)/shard_map/convert_element_type | solution.py:71
  (24 shorter events, 2.9 us)
Async XLA Ops:
  22.7 17.7 %all-to-all-start = ((bf16[16,24,4,128]{3,2,1,0:T(4,128)(2,1)}), bf16[16,24,4,128]{3,2,1,0:T(4,128)(2,1)S(1)}, u32[]{:S(2)}, u32[]{:S(2)}) async-start(bf16[16,24,4,128]{3,2,1,0:T(4,128)(2,1)} %constant_dynamic-update-slice_fusion), calls=%async_computation | async-start | bytes 786432 | tf_op jit(solution)/shard_map/all_to_all | solution.py:61
  29.3 11.2 %copy-start = (bf16[4,4,384,192]{2,3,1,0:T(8,128)(2,1)S(1)}, bf16[4,4,384,192]{2,3,1,0:T(8,128)(2,1)}, u32[]{:S(2)}) copy-start(bf16[4,4,384,192]{2,3,1,0:T(8,128)(2,1)} %param.8) | copy-start | bytes 7077892
  41.1 5.4 %collective-permute-start = (bf16[384,1,128]{2,0,1:T(8,128)(2,1)S(1)}, bf16[384,1,128]{2,0,1:T(8,128)(2,1)S(1)}, u32[]{:S(2)}, u32[]{:S(2)}) collective-permute-start(bf16[384,1,128]{2,0,1:T(8,128)(2,1)S(1)} %get-tuple-element.7), channel_id=1, source_target_pairs={{0,1},{1,2},{2,3},{3,4},{4,5},{5,6},{6,7},{7,8},{8,9},{9,10},{10,1... | collective-permute-start | bytes 294920 | tf_op jit(solution)/shard_map/ppermute | solution.py:16
  44.3 6.8 %collective-permute-start.1 = (bf16[384,1,128]{2,0,1:T(8,128)(2,1)S(1)}, bf16[384,1,128]{2,0,1:T(8,128)(2,1)S(1)}, u32[]{:S(2)}, u32[]{:S(2)}) collective-permute-start(bf16[384,1,128]{2,0,1:T(8,128)(2,1)S(1)} %get-tuple-element.8), channel_id=1, source_target_pairs={{1,0},{2,1},{3,2},{4,3},{5,4},{6,5},{7,6},{8,7},{9,8},{10,9},{11,1... | collective-permute-start | bytes 294920 | tf_op jit(solution)/shard_map/ppermute | solution.py:17
  62.4 1.9 %copy-start.2 = (f32[192]{0:T(256)S(1)}, f32[192]{0:T(256)}, u32[]{:S(2)}) copy-start(f32[192]{0:T(256)} %param.9) | copy-start | bytes 2308
  64.5 4.7 %copy-start.1 = (bf16[3,3,384,192]{2,3,1,0:T(8,128)(2,1)S(1)}, bf16[3,3,384,192]{2,3,1,0:T(8,128)(2,1)}, u32[]{:S(2)}) copy-start(bf16[3,3,384,192]{2,3,1,0:T(8,128)(2,1)} %param.10) | copy-start | bytes 3981316
  64.5 5.2 %collective-permute-start.2 = (bf16[384,1,256]{2,0,1:T(8,128)(2,1)S(1)}, bf16[384,1,256]{2,0,1:T(8,128)(2,1)S(1)}, u32[]{:S(2)}, u32[]{:S(2)}) collective-permute-start(bf16[384,1,256]{2,0,1:T(8,128)(2,1)S(1)} %get-tuple-element.5), channel_id=1, source_target_pairs={{0,1},{1,2},{2,3},{3,4},{4,5},{5,6},{6,7},{7,8},{8,9},{9,10},{10,1... | collective-permute-start | bytes 589832 | tf_op jit(solution)/shard_map/ppermute | solution.py:16
  66.6 7.9 %collective-permute-start.3 = (bf16[384,1,256]{2,0,1:T(8,128)(2,1)S(1)}, bf16[384,1,256]{2,0,1:T(8,128)(2,1)S(1)}, u32[]{:S(2)}, u32[]{:S(2)}) collective-permute-start(bf16[384,1,256]{2,0,1:T(8,128)(2,1)S(1)} %get-tuple-element.6), channel_id=1, source_target_pairs={{1,0},{2,1},{3,2},{4,3},{5,4},{6,5},{7,6},{8,7},{9,8},{10,9},{11,1... | collective-permute-start | bytes 589832 | tf_op jit(solution)/shard_map/ppermute | solution.py:17
  81.7 0.7 copy-start.3
